TPU v7x, 128 devices: a whole 4x4x4 slice. The times are simulated.
128 devices in a mesh: node: 4 (over x), ep: 32 (over y, z, core).
Axes of the slice: x: 4, y: 4, z: 4, core: 2. Of those that a mesh axis runs over, the one named last changes fastest.
Arguments:
- images: bfloat16 [128, 257, 1280], P(('node', 'ep')), may hold values from -6 to 6
- w_query: bfloat16 [1280, 1280], P(None, 'node'), may hold values from -6 to 6
- w_key: bfloat16 [1280, 1280], P(None, 'node'), may hold values from -6 to 6
- w_value: bfloat16 [1280, 1280], P(None, 'node'), may hold values from -0.15625 to 0.15625
- w_output: bfloat16 [1280, 1280], replicated, may hold values from -0.15625 to 0.15625
- router: bfloat16 [1280, 32], replicated, may hold values from -0.15625 to 0.15625
- w_in: bfloat16 [32, 1280, 5120], P('ep', None, 'node'), may hold values from -0.15625 to 0.15625
- w_out: bfloat16 [32, 5120, 1280], P('ep', 'node'), may hold values from -0.078125 to 0.078125
- routes: int32 [128, 257, 2], P(('node', 'ep')), may hold values from 0 to 31, all different within a row; in each aligned block of 257 rows (0 to 256, 257 to 513, ..., all dimensions but the last counted through in order) at most 24 rows name the same one
Outputs:
- output: bfloat16 [128, 257, 1280], P(('node', 'ep'))
Inputs may be any that keep to these rules, and one draw needn't show every extreme that they name: `routes`: the two experts of a token differ. At most 24 tokens of one image name the same expert, and in every draw some image has an expert named by exactly 24 of its tokens.
All inputs are finite; a program needn't handle non-finite values.
Results may differ from a plain program's by a relative error of at most 0.0085.
Values may be sent and summed in bfloat16 or wider, within the bound.
No kernel may reach another device: no remote copies, remote signals or barrier semaphores. Data moves between devices by JAX's collectives and lax.ppermute only.
A program may use at most 128 MiB of HBM per device.

v0:
```python
import math
import jax
import jax.numpy as jnp
from jax import lax
from jax.sharding import PartitionSpec as P

D = 1280
HEADS = 16
CAP = 24


def layer_norm(values):
    center = values - jnp.mean(values, axis=-1, keepdims=True)
    spread = jnp.mean(center * center, axis=-1, keepdims=True)
    return center * lax.rsqrt(spread + 1e-06)


def slot_table(chosen, num_experts):
    onehot = (chosen[..., None] == jnp.arange(num_experts, dtype=jnp.int32)).astype(jnp.int32)
    before = jnp.cumsum(onehot, axis=1) - onehot
    return jnp.sum(before * onehot, axis=-1)


def shards(images, w_query, w_key, w_value, w_output, router, w_in, w_out, routes):
    local_images, tokens_dev, width = images.shape
    head_size = D // HEADS
    local_heads = w_query.shape[1] // head_size
    node_count = lax.axis_size("node")
    column_count = lax.axis_size("ep")
    num_experts = router.shape[1]
    local_experts = w_in.shape[0]
    slot_count = local_images * CAP
    inputs = images.astype(jnp.float32)
    normed = layer_norm(inputs).astype(jnp.bfloat16)
    shard_rows = lax.all_gather(normed, "node", axis=0, tiled=True)
    number = shard_rows.shape[0]
    queries = jnp.einsum(
        "ctd,de->cte", shard_rows, w_query, preferred_element_type=jnp.float32
    ).astype(jnp.bfloat16)
    projected_keys = jnp.einsum(
        "ctd,de->cte", shard_rows, w_key, preferred_element_type=jnp.float32
    ).astype(jnp.bfloat16)
    projected_values = jnp.einsum(
        "ctd,de->cte", shard_rows, w_value, preferred_element_type=jnp.float32
    ).astype(jnp.bfloat16)
    query_heads = queries.reshape(number, tokens_dev, local_heads, head_size)
    key_heads = projected_keys.reshape(number, tokens_dev, local_heads, head_size)
    value_heads = projected_values.reshape(number, tokens_dev, local_heads, head_size)
    scores = jnp.einsum(
        "cqhd,ckhd->chqk", query_heads, key_heads, preferred_element_type=jnp.float32
    ) / math.sqrt(head_size)
    weights = jax.nn.softmax(scores, axis=-1).astype(jnp.bfloat16)
    mixture = jnp.einsum(
        "chqk,ckhd->cqhd", weights, value_heads, preferred_element_type=jnp.float32
    ).astype(jnp.bfloat16)
    head_results = mixture.reshape(number, tokens_dev, local_heads * head_size)
    attention = jnp.einsum(
        "itd,de->ite",
        lax.all_to_all(head_results, "node", split_axis=0, concat_axis=2, tiled=True),
        w_output,
        preferred_element_type=jnp.float32,
    )
    middle = inputs + attention
    normed_second = layer_norm(middle).astype(jnp.bfloat16)
    logits = jnp.einsum("itd,de->ite", normed_second, router, preferred_element_type=jnp.float32)
    chosen_mask = routes[..., None] == jnp.arange(num_experts, dtype=jnp.int32)
    chosen_logit = jnp.sum(jnp.where(chosen_mask, logits[:, :, None, :], jnp.float32(0.0)), axis=-1)
    gate_values = jax.nn.sigmoid(chosen_logit)
    flat_routes = routes.reshape(local_images, 2 * tokens_dev)
    slot_index = slot_table(flat_routes, num_experts)
    image_base = jnp.arange(local_images, dtype=jnp.int32)[:, None] * CAP
    position = (flat_routes * slot_count + image_base + slot_index).reshape(-1)
    token_ids = jnp.arange(local_images * 2 * tokens_dev, dtype=jnp.int32) // 2
    source = jnp.full((num_experts * slot_count,), -1, jnp.int32).at[position].set(token_ids)
    token_rows = normed_second.reshape(local_images * tokens_dev, width)
    gathered = jnp.take(token_rows, jnp.maximum(source, 0), axis=0)
    gathered = jnp.where(source[:, None] >= 0, gathered, jnp.zeros_like(gathered))
    outgoing = gathered.reshape(column_count, local_experts, slot_count, width)
    copies = jnp.broadcast_to(outgoing[None], (node_count,) + outgoing.shape)
    copies = copies.reshape(node_count * column_count, local_experts, slot_count, width)
    arrived = lax.all_to_all(copies, ("node", "ep"), split_axis=0, concat_axis=0, tiled=True)
    pre_act = jnp.einsum("lesd,edf->lesf", arrived, w_in, preferred_element_type=jnp.float32)
    hidden = jax.nn.gelu(pre_act, approximate=True).astype(jnp.bfloat16)
    partial_sum = jnp.einsum(
        "lesf,efd->lesd", hidden, w_out, preferred_element_type=jnp.float32
    ).astype(jnp.bfloat16)
    returned = lax.all_to_all(partial_sum, ("node", "ep"), split_axis=0, concat_axis=0, tiled=True)
    returned = returned.astype(jnp.float32).reshape(
        node_count, column_count, local_experts, slot_count, width
    )
    expert_result = jnp.sum(returned, axis=0).astype(jnp.bfloat16)
    result_rows = expert_result.reshape(num_experts * slot_count, width)
    picked = jnp.take(result_rows, position, axis=0).reshape(local_images, tokens_dev, 2, width)
    expert_mix = jnp.sum(gate_values[..., None] * picked.astype(jnp.float32), axis=2)
    return (middle + expert_mix).astype(jnp.bfloat16)


def solution(mesh):
    placed = (
        P(("node", "ep"), None, None),
        P(None, "node"),
        P(None, "node"),
        P(None, "node"),
        P(),
        P(),
        P("ep", None, "node"),
        P("ep", "node", None),
        P(("node", "ep"), None, None),
    )
    return jax.shard_map(
        shards, mesh=mesh, in_specs=placed, out_specs=P(("node", "ep"), None, None), check_vma=False
    )
```

profile of v0, /device:TPU:97, one launch (start us, length us, event | category | flops | bytes accessed | tf_op | source)
XLA Modules:
  0.0 396.5 jit_solution(17544285698891339135)
XLA Ops:
  15.9 4.1 %scatter_custom_fusion = s32[768]{0:T(1024)S(1)} fusion(s32[514]{0:T(1024)S(1)} %fusion.49, s32[514]{0:T(1024)S(1)} %add_select_fusion, s32[]{:T(128)} %constant.77.clone.1), kind=kCustom, calls=%fused_computation.80 | custom fusion | bytes 3076 | tf_op jit(solution)/shard_map/scatter | solution.py:74
  20.0 28.8 %all-gather.2.cloned.1.call-done = bf16[4,257,1280]{2,1,0:T(8,128)(2,1)} async-done(((bf16[1,257,1280]{2,1,0:T(8,128)(2,1)}), bf16[4,257,1280]{2,1,0:T(8,128)(2,1)}) %all-gather.2.cloned.1.call-update) | async-done | bytes 2631696 | tf_op jit(solution)/shard_map/all_gather | solution.py:35
  48.8 4.4 %convolution_convert_fusion = bf16[4,257,320]{2,1,0:T(8,128)(2,1)} fusion(bf16[4,257,1280]{2,1,0:T(8,128)(2,1)} %all-gather.2.cloned.1.call-done, bf16[1280,320]{0,1:T(8,128)(2,1)} %param.11), kind=kOutput, calls=%fused_computation.37 | convolution fusion | flops 842466560 | bytes 4108800 | tf_op jit(solution)/shard_map/ctd,de->cte/dot_general | solution.py:40
  53.2 2.3 copy.95
  55.5 4.4 %convolution_convert_fusion.2 = bf16[4,257,320]{2,1,0:T(8,128)(2,1)} fusion(bf16[4,257,1280]{2,1,0:T(8,128)(2,1)} %all-gather.2.cloned.1.call-done, bf16[1280,320]{0,1:T(8,128)(2,1)} %param.12), kind=kOutput, calls=%fused_computation.39 | convolution fusion | flops 842466560 | bytes 4108800 | tf_op jit(solution)/shard_map/ctd,de->cte/dot_general | solution.py:43
  62.2 4.4 %convolution_convert_fusion.1 = bf16[4,257,320]{2,1,0:T(8,128)(2,1)} fusion(bf16[4,257,1280]{2,1,0:T(8,128)(2,1)} %all-gather.2.cloned.1.call-done, bf16[1280,320]{0,1:T(8,128)(2,1)} %param.10), kind=kOutput, calls=%fused_computation.38 | convolution fusion | flops 842466560 | bytes 4108800 | tf_op jit(solution)/shard_map/ctd,de->cte/dot_general | solution.py:37
  66.6 2.3 copy.94
  68.9 6.5 %fusion.57 = (f32[4,4,257]{2,1,0:T(4,128)S(1)}, f32[4,4,257,257]{2,3,1,0:T(8,128)}) fusion(bf16[4,257,4,80]{1,3,2,0:T(8,128)(2,1)} %bitcast.114, bf16[4,257,4,80]{1,3,2,0:T(8,128)(2,1)} %bitcast.113), kind=kOutput, calls=%fused_computation.92 | convolution fusion | flops 172256048 | bytes 5559424 | tf_op jit(solution)/shard_map/sub | solution.py:52
  75.4 5.1 %fusion.33 = bf16[4,4,80,257]{3,2,1,0:T(8,128)(2,1)} fusion(bf16[4,257,4,80]{1,3,2,0:T(8,128)(2,1)} %bitcast.112, f32[4,4,257,257]{2,3,1,0:T(8,128)} %get-tuple-element.8, f32[4,4,257]{2,1,0:T(4,128)S(1)} %get-tuple-element.7), kind=kOutput, calls=%fused_computation.36 | convolution fusion | flops 171527968 | bytes 5559424 | tf_op jit(solution)/shard_map/chqk,ckhd->cqhd/dot_general | solution.py:53
  82.8 4.4 %all-to-all-start = ((bf16[4,257,320]{2,1,0:T(8,128)(2,1)}), bf16[4,257,320]{2,1,0:T(8,128)(2,1)}, u32[]{:S(2)}, u32[]{:S(2)}) async-start(bf16[4,257,320]{2,1,0:T(8,128)(2,1)} %copy.97), calls=%async_computation | async-start | bytes 1622016 | tf_op jit(solution)/shard_map/all_to_all | solution.py:59
  87.4 11.5 %all-to-all-done = bf16[4,257,320]{2,1,0:T(8,128)(2,1)} async-done(((bf16[4,257,320]{2,1,0:T(8,128)(2,1)}), bf16[4,257,320]{2,1,0:T(8,128)(2,1)}, u32[]{:S(2)}, u32[]{:S(2)}) %all-to-all-start) | async-done | bytes 657952 | tf_op jit(solution)/shard_map/all_to_all | solution.py:59
  98.8 2.3 copy.98
  101.2 2.5 reshape.358
  103.7 3.4 fusion.58
  109.3 6.4 %gather_fusion = bf16[768,1280]{1,0:T(8,128)(2,1)} fusion(bf16[257,1280]{1,0:T(8,128)(2,1)} %fusion.40, s32[1024]{0:T(1024)S(1)} %pad_clamp_fusion.1), kind=kCustom, calls=%fused_computation | custom fusion | bytes 3935232 | tf_op jit(solution)/shard_map/jit(_take)/gather | solution.py:76
  118.1 99.0 %all_to_all.25 = bf16[128,1,24,1280]{3,2,1,0:T(8,128)(2,1)} all-to-all(bf16[128,1,24,1280]{3,2,1,0:T(8,128)(2,1)S(1)} %bitcast.110), channel_id=1, replica_groups=mesh['node'=4,'ep'=32] {'node','ep'}, dimensions={0} | all-to-all | bytes 15728640 | tf_op jit(solution)/shard_map/all_to_all | solution.py:81
  217.1 25.9 %convert_bitcast_fusion = bf16[128,1,24,1280]{3,0,2,1:T(8,128)(2,1)} fusion(bf16[1,1280,1280]{2,1,0:T(8,128)(2,1)S(1)} %copy-done, bf16[128,1,24,1280]{3,2,1,0:T(8,128)(2,1)} %all_to_all.25, bf16[1,1280,1280]{2,1,0:T(8,128)(2,1)} %param.15), kind=kOutput, calls=%fused_computation.18 | convolution fusion | flops 20171980800 | bytes 22282240 | tf_op jit(solution)/shard_map/lesf,efd->lesd/dot_general | solution.py:84
  243.0 10.8 %copy.108 = bf16[128,1,24,1280]{3,2,1,0:T(8,128)(2,1)} copy(bf16[128,1,24,1280]{3,0,2,1:T(8,128)(2,1)} %convert_bitcast_fusion) | data formatting | bytes 15728640 | tf_op jit(solution)/shard_map/convert_element_type | solution.py:86
  253.8 10.7 %all-to-all-start.2 = ((bf16[128,1,24,1280]{3,2,1,0:T(8,128)(2,1)}), bf16[128,1,24,1280]{3,2,1,0:T(8,128)(2,1)}, u32[]{:S(2)}, u32[]{:S(2)}) async-start(bf16[128,1,24,1280]{3,2,1,0:T(8,128)(2,1)} %copy.108), calls=%async_computation.2 | async-start | bytes 15728640 | tf_op jit(solution)/shard_map/all_to_all | solution.py:87
  265.5 97.6 %all-to-all-done.2 = bf16[128,1,24,1280]{3,2,1,0:T(8,128)(2,1)} async-done(((bf16[128,1,24,1280]{3,2,1,0:T(8,128)(2,1)}), bf16[128,1,24,1280]{3,2,1,0:T(8,128)(2,1)}, u32[]{:S(2)}, u32[]{:S(2)}) %all-to-all-start.2) | async-done | bytes 7864352 | tf_op jit(solution)/shard_map/all_to_all | solution.py:87
  363.1 4.3 %bitcast_reduce_fusion = bf16[32,24,1280]{2,1,0:T(8,128)(2,1)S(1)} fusion(bf16[4,32,24,1280]{3,2,1,0:T(8,128)(2,1)} %bitcast.107), kind=kLoop, calls=%fused_computation.13 | loop fusion | flops 2949120 | bytes 9830400 | tf_op jit(solution)/shard_map/reduce_sum | solution.py:91
  367.4 3.5 gather_fusion.1
  370.9 4.1 %gather.15 = bf16[1,257,2,1280]{3,2,1,0:T(2,128)(2,1)} reshape(bf16[514,1280]{1,0:T(8,128)(2,1)} %gather_fusion.1) | data formatting | bytes 2631680 | tf_op jit(solution)/shard_map/jit(_take)/gather | solution.py:93
  375.0 13.6 %multiply_reduce_fusion.1 = f32[257,1280]{1,0:T(8,128)S(1)} fusion(bf16[1,257,2,1280]{3,2,1,0:T(2,128)(2,1)} %gather.15, pred[257,2]{1,0:T(8,128)(4,1)S(1)} %copy.105, f32[257,2]{1,0:T(8,128)S(1)} %copy.99), kind=kLoop, calls=%fused_computation.29 | loop fusion | flops 2302720 | bytes 2634250 | tf_op jit(solution)/shard_map/reduce_sum | solution.py:94
  (63 shorter events, 20.4 us)
Async XLA Ops:
  6.5 210.6 %copy-start = (bf16[1,1280,1280]{2,1,0:T(8,128)(2,1)S(1)}, bf16[1,1280,1280]{2,1,0:T(8,128)(2,1)}, u32[]{:S(2)}) copy-start(bf16[1,1280,1280]{2,1,0:T(8,128)(2,1)} %param.16) | copy-start | bytes 9830404
  6.5 5.2 %copy-start.6 = (s32[1,257,2]{1,2,0:T(2,128)S(1)}, s32[1,257,2]{1,2,0:T(2,128)}, u32[]{:S(2)}) copy-start(s32[1,257,2]{1,2,0:T(2,128)} %param.17) | copy-start | bytes 6172
  6.5 42.2 %all-gather.2.cloned.1.call-start = ((), (), s32[]{:S(2)}) async-start(), calls=%async_computation.3 | async-start | bytes 3379200 | tf_op jit(solution)/shard_map/all_gather | solution.py:35
  82.8 16.1 %all-to-all-start = ((bf16[4,257,320]{2,1,0:T(8,128)(2,1)}), bf16[4,257,320]{2,1,0:T(8,128)(2,1)}, u32[]{:S(2)}, u32[]{:S(2)}) async-start(bf16[4,257,320]{2,1,0:T(8,128)(2,1)} %copy.97), calls=%async_computation | async-start | bytes 1622016 | tf_op jit(solution)/shard_map/all_to_all | solution.py:59
  107.2 1.1 copy-start.3
  253.8 11.2 %copy-start.2 = (bf16[257,1280]{1,0:T(8,128)(2,1)S(1)}, bf16[257,1280]{1,0:T(8,128)(2,1)}, u32[]{:S(2)}) copy-start(bf16[257,1280]{1,0:T(8,128)(2,1)} %fusion.40) | copy-start | bytes 1973764
  253.8 11.2 %copy-start.5 = (bf16[1280,32]{0,1:T(8,128)(2,1)S(1)}, bf16[1280,32]{0,1:T(8,128)(2,1)}, u32[]{:S(2)}) copy-start(bf16[1280,32]{0,1:T(8,128)(2,1)} %param.14) | copy-start | bytes 245764
  253.8 109.4 %all-to-all-start.2 = ((bf16[128,1,24,1280]{3,2,1,0:T(8,128)(2,1)}), bf16[128,1,24,1280]{3,2,1,0:T(8,128)(2,1)}, u32[]{:S(2)}, u32[]{:S(2)}) async-start(bf16[128,1,24,1280]{3,2,1,0:T(8,128)(2,1)} %copy.108), calls=%async_computation.2 | async-start | bytes 15728640 | tf_op jit(solution)/shard_map/all_to_all | solution.py:87
  370.9 18.7 %copy-start.1 = (bf16[1,1280,1280]{2,1,0:T(8,128)(2,1)S(1)}, bf16[1,1280,1280]{2,1,0:T(8,128)(2,1)}, u32[]{:S(2)}) copy-start(bf16[1,1280,1280]{2,1,0:T(8,128)(2,1)} %param.16) | copy-start | bytes 9830404
  375.0 13.6 %copy-start.4 = (f32[1,257,1280]{2,1,0:T(8,128)S(1)}, f32[1,257,1280]{2,1,0:T(8,128)}, u32[]{:S(2)}) copy-start(f32[1,257,1280]{2,1,0:T(8,128)} %copy-done.3) | copy-start | bytes 3947524
Sparse Core Ops, SparseCore 0:
  11.8 36.8 all-gather.1
where the time goes:
time: 397 us; the launch traced here: 396 us
  waiting for transfers between devices  138 us (35%)
  blocking collectives  99 us (25%)
  matrix products  54.6 us (14%)
  local copies, waits for them, and re-layouts  46.4 us (12%)
  other arithmetic  29.8 us (8%)
  starting transfers between devices  15.1 us (4%)
  between operations  13.7 us (3%)
    all_to_all x1, blocking collectives, shards(): lax.all_to_all(copies, ('node', 'ep'), split_axis=0, concat_axis=0, tiled...  99 us
    all_to_all x1, waiting for transfers between devices, shards(): lax.all_to_all(partial_sum, ('node', 'ep'), split_axis=0, concat_axis=0,...  97.6 us
    all_gather x1, waiting for transfers between devices, shards(): shard_rows = lax.all_gather(normed, 'node', axis=0, tiled=True)  28.8 us
    dot_general x1, matrix products, shards(): jnp.einsum('lesf,efd->lesd', hidden, w_out, preferred_element_type=jnp.fl...  25.9 us
    reduce_sum x1, other arithmetic, shards(): jnp.sum(gate_values[..., None] * picked.astype(jnp.float32), axis=2)  13.6 us
    all_to_all x1, waiting for transfers between devices, shards(): lax.all_to_all(head_results, 'node', split_axis=0, concat_axis=2, tiled=T...  11.5 us
    convert_element_type x1, local copies, waits for them, and re-layouts, shards(): partial_sum = jnp.einsum('lesf,efd->lesd', hidden, w_out, preferred_eleme...  10.8 us
    all_to_all x1, starting transfers between devices, shards(): lax.all_to_all(partial_sum, ('node', 'ep'), split_axis=0, concat_axis=0,...  10.7 us
  transfers between devices with their start and end apart: 3, of which 3 were waited for; matrix products, arithmetic and copies ran while one was open for 2% of the time, Pallas kernels for 0%

commit v1 on v0

--- a/solution.py
+++ b/solution.py
@@ -32,7 +32,14 @@
     slot_count = local_images * CAP
     inputs = images.astype(jnp.float32)
     normed = layer_norm(inputs).astype(jnp.bfloat16)
-    shard_rows = lax.all_gather(normed, "node", axis=0, tiled=True)
+    q_n = jax.lax.axis_size("node")
+    trail = []
+    for idx in range(normed.ndim):
+        trail.append(q_n if idx == 0 else 1)
+    wide_out = jnp.tile(normed, trail)
+    shard_rows = jax.lax.all_to_all(
+        wide_out, axis_name="node", split_axis=0, concat_axis=0, tiled=True
+    )
     number = shard_rows.shape[0]
     queries = jnp.einsum(
         "ctd,de->cte", shard_rows, w_query, preferred_element_type=jnp.float32

time: 397 us -> 385 us (0.970)
  between operations: 13.7 us -> 0.32 us
  waiting for transfers between devices: 138 us -> 132 us
  starting transfers between devices: 15.1 us -> 19.8 us
    all_gather x1 -> x0, waiting for transfers between devices: 28.8 us -> none  [shards(): shard_rows = lax.all_gather(normed, 'node', axis=0, tiled=True)]
    all_to_all x0 -> x1, waiting for transfers between devices: none -> 24 us  [shards(): jax.lax.all_to_all(wide_out, axis_name='node', split_axis=0, concat_axis=...]
    all_to_all x0 -> x1, starting transfers between devices: none -> 4.7 us  [shards(): jax.lax.all_to_all(wide_out, axis_name='node', split_axis=0, concat_axis=...]
where the time goes in v1:
time: 385 us; the launch traced here: 384 us
  waiting for transfers between devices  132 us (34%)
  blocking collectives  99.7 us (26%)
  matrix products  54.6 us (14%)
  local copies, waits for them, and re-layouts  48.1 us (12%)
  other arithmetic  29 us (8%)
  starting transfers between devices  19.8 us (5%)
    all_to_all x1, blocking collectives, shards(): lax.all_to_all(copies, ('node', 'ep'), split_axis=0, concat_axis=0, tiled...  99.7 us
    all_to_all x1, waiting for transfers between devices, shards(): lax.all_to_all(partial_sum, ('node', 'ep'), split_axis=0, concat_axis=0,...  97.6 us
    dot_general x1, matrix products, shards(): jnp.einsum('lesf,efd->lesd', hidden, w_out, preferred_element_type=jnp.fl...  25.9 us
    all_to_all x1, waiting for transfers between devices, shards(): jax.lax.all_to_all(wide_out, axis_name='node', split_axis=0, concat_axis=...  24 us
    reduce_sum x1, other arithmetic, shards(): jnp.sum(gate_values[..., None] * picked.astype(jnp.float32), axis=2)  13.6 us
    all_to_all x1, waiting for transfers between devices, shards(): lax.all_to_all(head_results, 'node', split_axis=0, concat_axis=2, tiled=T...  10.8 us
    convert_element_type x1, local copies, waits for them, and re-layouts, shards(): partial_sum = jnp.einsum('lesf,efd->lesd', hidden, w_out, preferred_eleme...  10.8 us
    all_to_all x1, starting transfers between devices, shards(): lax.all_to_all(partial_sum, ('node', 'ep'), split_axis=0, concat_axis=0,...  10.7 us
  transfers between devices with their start and end apart: 3, of which 3 were waited for; matrix products, arithmetic and copies ran while one was open for 2% of the time, Pallas kernels for 0%

profile of v1, /device:TPU:97, one launch (start us, length us, event | category | flops | bytes accessed | tf_op | source)
XLA Modules:
  0.0 383.9 jit_solution(10894553052858725679)
XLA Ops:
  6.0 4.7 %all-to-all-start = ((bf16[4,257,1280]{2,1,0:T(8,128)(2,1)}), bf16[4,257,1280]{2,1,0:T(8,128)(2,1)}, u32[]{:S(2)}, u32[]{:S(2)}) async-start(bf16[4,257,1280]{2,1,0:T(8,128)(2,1)} %tile.10), calls=%async_computation | async-start | bytes 5406720 | tf_op jit(solution)/shard_map/all_to_all | solution.py:40
  14.9 4.1 %scatter_custom_fusion = s32[768]{0:T(1024)S(1)} fusion(s32[514]{0:T(1024)S(1)} %fusion.50, s32[514]{0:T(1024)S(1)} %add_select_fusion, s32[]{:T(128)} %constant.77.clone.1), kind=kCustom, calls=%fused_computation.81 | custom fusion | bytes 3076 | tf_op jit(solution)/shard_map/scatter | solution.py:81
  19.0 24.0 %all-to-all-done = bf16[4,257,1280]{2,1,0:T(8,128)(2,1)} async-done(((bf16[4,257,1280]{2,1,0:T(8,128)(2,1)}), bf16[4,257,1280]{2,1,0:T(8,128)(2,1)}, u32[]{:S(2)}, u32[]{:S(2)}) %all-to-all-start) | async-done | bytes 2631712 | tf_op jit(solution)/shard_map/all_to_all | solution.py:40
  43.0 4.4 %convolution_convert_fusion = bf16[4,257,320]{2,1,0:T(8,128)(2,1)} fusion(bf16[4,257,1280]{2,1,0:T(8,128)(2,1)} %all-to-all-done, bf16[1280,320]{0,1:T(8,128)(2,1)} %param.11), kind=kOutput, calls=%fused_computation.37 | convolution fusion | flops 842466560 | bytes 4108800 | tf_op jit(solution)/shard_map/ctd,de->cte/dot_general | solution.py:47
  49.8 4.4 %convolution_convert_fusion.2 = bf16[4,257,320]{2,1,0:T(8,128)(2,1)} fusion(bf16[4,257,1280]{2,1,0:T(8,128)(2,1)} %all-to-all-done, bf16[1280,320]{0,1:T(8,128)(2,1)} %param.12), kind=kOutput, calls=%fused_computation.39 | convolution fusion | flops 842466560 | bytes 4108800 | tf_op jit(solution)/shard_map/ctd,de->cte/dot_general | solution.py:50
  56.4 4.4 %convolution_convert_fusion.1 = bf16[4,257,320]{2,1,0:T(8,128)(2,1)} fusion(bf16[4,257,1280]{2,1,0:T(8,128)(2,1)} %all-to-all-done, bf16[1280,320]{0,1:T(8,128)(2,1)} %param.10), kind=kOutput, calls=%fused_computation.38 | convolution fusion | flops 842466560 | bytes 4108800 | tf_op jit(solution)/shard_map/ctd,de->cte/dot_general | solution.py:44
  60.9 2.3 copy.94
  63.2 6.5 %fusion.58 = (f32[4,4,257]{2,1,0:T(4,128)S(1)}, f32[4,4,257,257]{2,3,1,0:T(8,128)}) fusion(bf16[4,257,4,80]{1,3,2,0:T(8,128)(2,1)} %bitcast.116, bf16[4,257,4,80]{1,3,2,0:T(8,128)(2,1)} %bitcast.115), kind=kOutput, calls=%fused_computation.93 | convolution fusion | flops 172256048 | bytes 5559424 | tf_op jit(solution)/shard_map/sub | solution.py:59
  69.7 5.1 %fusion.33 = bf16[4,4,80,257]{3,2,1,0:T(8,128)(2,1)} fusion(bf16[4,257,4,80]{1,3,2,0:T(8,128)(2,1)} %bitcast.114, f32[4,4,257,257]{2,3,1,0:T(8,128)} %get-tuple-element.8, f32[4,4,257]{2,1,0:T(4,128)S(1)} %get-tuple-element.7), kind=kOutput, calls=%fused_computation.36 | convolution fusion | flops 171527968 | bytes 5559424 | tf_op jit(solution)/shard_map/chqk,ckhd->cqhd/dot_general | solution.py:60
  77.0 4.4 %all-to-all-start.1 = ((bf16[4,257,320]{2,1,0:T(8,128)(2,1)}), bf16[4,257,320]{2,1,0:T(8,128)(2,1)}, u32[]{:S(2)}, u32[]{:S(2)}) async-start(bf16[4,257,320]{2,1,0:T(8,128)(2,1)} %copy.97), calls=%async_computation.1 | async-start | bytes 1622016 | tf_op jit(solution)/shard_map/all_to_all | solution.py:66
  81.6 10.8 %all-to-all-done.1 = bf16[4,257,320]{2,1,0:T(8,128)(2,1)} async-done(((bf16[4,257,320]{2,1,0:T(8,128)(2,1)}), bf16[4,257,320]{2,1,0:T(8,128)(2,1)}, u32[]{:S(2)}, u32[]{:S(2)}) %all-to-all-start.1) | async-done | bytes 657952 | tf_op jit(solution)/shard_map/all_to_all | solution.py:66
  92.4 2.3 copy.98
  94.7 2.5 reshape.361
  97.3 3.4 fusion.59
  102.9 6.4 %gather_fusion = bf16[768,1280]{1,0:T(8,128)(2,1)} fusion(bf16[257,1280]{1,0:T(8,128)(2,1)} %fusion.40, s32[1024]{0:T(1024)S(1)} %pad_clamp_fusion.1), kind=kCustom, calls=%fused_computation | custom fusion | bytes 3935232 | tf_op jit(solution)/shard_map/jit(_take)/gather | solution.py:83
  111.6 99.7 %all_to_all.30 = bf16[128,1,24,1280]{3,2,1,0:T(8,128)(2,1)} all-to-all(bf16[128,1,24,1280]{3,2,1,0:T(8,128)(2,1)S(1)} %bitcast.112), channel_id=1, replica_groups=mesh['node'=4,'ep'=32] {'node','ep'}, dimensions={0} | all-to-all | bytes 15728640 | tf_op jit(solution)/shard_map/all_to_all | solution.py:88
  211.4 25.9 %convert_bitcast_fusion = bf16[128,1,24,1280]{3,0,2,1:T(8,128)(2,1)} fusion(bf16[1,1280,1280]{2,1,0:T(8,128)(2,1)S(1)} %copy-done, bf16[128,1,24,1280]{3,2,1,0:T(8,128)(2,1)} %all_to_all.30, bf16[1,1280,1280]{2,1,0:T(8,128)(2,1)} %param.15), kind=kOutput, calls=%fused_computation.18 | convolution fusion | flops 20171980800 | bytes 22282240 | tf_op jit(solution)/shard_map/lesf,efd->lesd/dot_general | solution.py:91
  237.2 10.8 %copy.108 = bf16[128,1,24,1280]{3,2,1,0:T(8,128)(2,1)} copy(bf16[128,1,24,1280]{3,0,2,1:T(8,128)(2,1)} %convert_bitcast_fusion) | data formatting | bytes 15728640 | tf_op jit(solution)/shard_map/convert_element_type | solution.py:93
  248.0 10.7 %all-to-all-start.3 = ((bf16[128,1,24,1280]{3,2,1,0:T(8,128)(2,1)}), bf16[128,1,24,1280]{3,2,1,0:T(8,128)(2,1)}, u32[]{:S(2)}, u32[]{:S(2)}) async-start(bf16[128,1,24,1280]{3,2,1,0:T(8,128)(2,1)} %copy.108), calls=%async_computation.3 | async-start | bytes 15728640 | tf_op jit(solution)/shard_map/all_to_all | solution.py:94
  259.7 97.6 %all-to-all-done.3 = bf16[128,1,24,1280]{3,2,1,0:T(8,128)(2,1)} async-done(((bf16[128,1,24,1280]{3,2,1,0:T(8,128)(2,1)}), bf16[128,1,24,1280]{3,2,1,0:T(8,128)(2,1)}, u32[]{:S(2)}, u32[]{:S(2)}) %all-to-all-start.3) | async-done | bytes 7864352 | tf_op jit(solution)/shard_map/all_to_all | solution.py:94
  357.4 4.3 %bitcast_reduce_fusion = bf16[32,24,1280]{2,1,0:T(8,128)(2,1)S(1)} fusion(bf16[4,32,24,1280]{3,2,1,0:T(8,128)(2,1)} %bitcast.109), kind=kLoop, calls=%fused_computation.13 | loop fusion | flops 2949120 | bytes 9830400 | tf_op jit(solution)/shard_map/reduce_sum | solution.py:98
  361.7 3.5 gather_fusion.1
  365.1 4.1 %gather.15 = bf16[1,257,2,1280]{3,2,1,0:T(2,128)(2,1)} reshape(bf16[514,1280]{1,0:T(8,128)(2,1)} %gather_fusion.1) | data formatting | bytes 2631680 | tf_op jit(solution)/shard_map/jit(_take)/gather | solution.py:100
  369.3 13.6 %multiply_reduce_fusion.1 = f32[257,1280]{1,0:T(8,128)S(1)} fusion(bf16[1,257,2,1280]{3,2,1,0:T(2,128)(2,1)} %gather.15, pred[257,2]{1,0:T(8,128)(4,1)S(1)} %copy.105, f32[257,2]{1,0:T(8,128)S(1)} %copy.99), kind=kLoop, calls=%fused_computation.29 | loop fusion | flops 2302720 | bytes 2634250 | tf_op jit(solution)/shard_map/reduce_sum | solution.py:101
  (63 shorter events, 23.5 us)
Async XLA Ops:
  0.0 211.4 %copy-start = (bf16[1,1280,1280]{2,1,0:T(8,128)(2,1)S(1)}, bf16[1,1280,1280]{2,1,0:T(8,128)(2,1)}, u32[]{:S(2)}) copy-start(bf16[1,1280,1280]{2,1,0:T(8,128)(2,1)} %param.16) | copy-start | bytes 9830404
  6.0 4.7 %copy-start.6 = (s32[1,257,2]{1,2,0:T(2,128)S(1)}, s32[1,257,2]{1,2,0:T(2,128)}, u32[]{:S(2)}) copy-start(s32[1,257,2]{1,2,0:T(2,128)} %param.17) | copy-start | bytes 6172
  6.0 37.0 %all-to-all-start = ((bf16[4,257,1280]{2,1,0:T(8,128)(2,1)}), bf16[4,257,1280]{2,1,0:T(8,128)(2,1)}, u32[]{:S(2)}, u32[]{:S(2)}) async-start(bf16[4,257,1280]{2,1,0:T(8,128)(2,1)} %tile.10), calls=%async_computation | async-start | bytes 5406720 | tf_op jit(solution)/shard_map/all_to_all | solution.py:40
  77.0 15.4 %all-to-all-start.1 = ((bf16[4,257,320]{2,1,0:T(8,128)(2,1)}), bf16[4,257,320]{2,1,0:T(8,128)(2,1)}, u32[]{:S(2)}, u32[]{:S(2)}) async-start(bf16[4,257,320]{2,1,0:T(8,128)(2,1)} %copy.97), calls=%async_computation.1 | async-start | bytes 1622016 | tf_op jit(solution)/shard_map/all_to_all | solution.py:66
  100.7 1.1 copy-start.3
  248.0 11.2 %copy-start.2 = (bf16[257,1280]{1,0:T(8,128)(2,1)S(1)}, bf16[257,1280]{1,0:T(8,128)(2,1)}, u32[]{:S(2)}) copy-start(bf16[257,1280]{1,0:T(8,128)(2,1)} %fusion.40) | copy-start | bytes 1973764
  248.0 11.2 %copy-start.5 = (bf16[1280,32]{0,1:T(8,128)(2,1)S(1)}, bf16[1280,32]{0,1:T(8,128)(2,1)}, u32[]{:S(2)}) copy-start(bf16[1280,32]{0,1:T(8,128)(2,1)} %param.14) | copy-start | bytes 245764
  248.0 109.4 %all-to-all-start.3 = ((bf16[128,1,24,1280]{3,2,1,0:T(8,128)(2,1)}), bf16[128,1,24,1280]{3,2,1,0:T(8,128)(2,1)}, u32[]{:S(2)}, u32[]{:S(2)}) async-start(bf16[128,1,24,1280]{3,2,1,0:T(8,128)(2,1)} %copy.108), calls=%async_computation.3 | async-start | bytes 15728640 | tf_op jit(solution)/shard_map/all_to_all | solution.py:94
  365.1 18.7 %copy-start.1 = (bf16[1,1280,1280]{2,1,0:T(8,128)(2,1)S(1)}, bf16[1,1280,1280]{2,1,0:T(8,128)(2,1)}, u32[]{:S(2)}) copy-start(bf16[1,1280,1280]{2,1,0:T(8,128)(2,1)} %param.16) | copy-start | bytes 9830404
  369.2 13.6 %copy-start.4 = (f32[1,257,1280]{2,1,0:T(8,128)S(1)}, f32[1,257,1280]{2,1,0:T(8,128)}, u32[]{:S(2)}) copy-start(f32[1,257,1280]{2,1,0:T(8,128)} %copy-done.3) | copy-start | bytes 3947524
